TPU v7x, 128 devices: a whole 4x4x4 slice. The times are simulated.
128 devices in a mesh: space: 8 (over z_hi, x), blk: 16 (over y, z_lo, core).
Axes of the slice: x: 4, y: 4, z: 4 (z_hi: 2, z_lo: 2; z = z_hi * 2 + z_lo), core: 2. Of those that a mesh axis runs over, the one named last changes fastest.
Arguments:
- density: bfloat16 [12288, 128, 128], P(('space', 'blk')), may hold values from -6 to 6
- bra_table: bfloat16 [12288, 128, 256], P(('space', 'blk')), may hold values from -0.5 to 0.5
- ket_table: bfloat16 [12288, 128, 256], P(('space', 'blk')), may hold values from -0.5 to 0.5
- box_of_block: int32 [12288], P(('space', 'blk')), may hold values from 0 to 127
- leaf_src: int32 [1024, 27], P(('space', 'blk')), may hold values from 0 to 383
- leaf_type: int32 [1024, 27], P(('space', 'blk')), may hold values from 0 to 15
- coarse_src: int32 [128, 27], P(('space', 'blk')), may hold values from 0 to 127
- coarse_type: int32 [128, 27], P(('space', 'blk')), may hold values from 0 to 15
- translation: float32 [16, 256, 256], replicated, may hold values from -0.375 to 0.375
- upward_translation_table: float32 [8, 256, 256], replicated, may hold values from -0.375 to 0.375
Outputs:
- coulomb: bfloat16 [12288, 128, 128], P(('space', 'blk'))
- box_locals: float32 [1024, 256], P(('space', 'blk'))
All inputs are finite; a program needn't handle non-finite values.
Results may differ from a plain program's by a relative error of at most 0.0049.
Values sent between devices are 32-bit elements; how exact they have to be, the bound alone decides.
No kernel may reach another device: no remote copies, remote signals or barrier semaphores. Data moves between devices by JAX's collectives and lax.ppermute only.
A program may use at most 128 MiB of HBM per device.

v0:
```python
import jax
import jax.numpy as jnp
from jax import lax
from jax.sharding import PartitionSpec as P


def padded(block, sides, width):
    for axis, dim in sides:
        count = lax.axis_size(axis)
        forward = [(i, i + 1) for i in range(count - 1)]
        backward = [(target, source) for source, target in forward]
        low = lax.ppermute(
            lax.slice_in_dim(block, block.shape[dim] - width, None, axis=dim), axis, forward
        )
        high = lax.ppermute(lax.slice_in_dim(block, 0, width, axis=dim), axis, backward)
        block = jnp.concatenate([low, block, high], axis=dim)
    return block


def shards(
    density,
    bra_table,
    ket_table,
    box_of_block,
    leaf_src,
    leaf_type,
    coarse_src,
    coarse_type,
    translation,
    upward_translation_table,
):
    top_level_index = lax.Precision.HIGHEST
    n_blk = lax.axis_size("blk")
    box_dom = 8 * n_blk
    n_types = translation.shape[0]
    inner = jnp.einsum("bmn,bmk->bnk", density, bra_table, preferred_element_type=jnp.float32)
    moments = jnp.sum(inner * ket_table.astype(jnp.float32), axis=1)
    box_hot = (box_of_block[:, None] == jnp.arange(box_dom, dtype=jnp.int32)[None, :]).astype(
        jnp.float32
    )
    partial_moments = lax.dot_general(
        box_hot, moments, (((0,), (0,)), ((), ())), precision=top_level_index
    )
    held_boxes = lax.psum_scatter(partial_moments, "blk", scatter_dimension=0, tiled=True)
    domain = lax.all_gather(held_boxes, "blk", axis=0, tiled=True)
    window = padded(domain, (("space", 0),), box_dom)
    self_parent_index = jnp.einsum(
        "oe,ode->d", held_boxes, upward_translation_table, precision=top_level_index
    )[None, :]
    all_parents = lax.all_gather(self_parent_index, ("space", "blk"), axis=0, tiled=True)
    src_hot = (leaf_src[..., None] == jnp.arange(3 * box_dom, dtype=jnp.int32)).astype(jnp.float32)
    type_hot = (leaf_type[..., None] == jnp.arange(n_types, dtype=jnp.int32)).astype(jnp.float32)
    counts = jnp.einsum("blt,blj->btj", type_hot, src_hot, precision=top_level_index)
    gathered = jnp.einsum("btj,jk->btk", counts, window, precision=top_level_index)
    leaf_far = jnp.einsum("btk,tlk->bl", gathered, translation, precision=top_level_index)
    n_parents = all_parents.shape[0]
    csrc_hot = (coarse_src[..., None] == jnp.arange(n_parents, dtype=jnp.int32)).astype(jnp.float32)
    ctype_hot = (coarse_type[..., None] == jnp.arange(n_types, dtype=jnp.int32)).astype(jnp.float32)
    ccounts = jnp.einsum("pet,peq->ptq", ctype_hot, csrc_hot, precision=top_level_index)
    cgathered = jnp.einsum("ptq,qk->ptk", ccounts, all_parents, precision=top_level_index)
    parent_local_expansion = jnp.einsum(
        "ptk,tlk->pl", cgathered, translation, precision=top_level_index
    )
    downward_sent = jnp.einsum(
        "d,uds->us", parent_local_expansion[0], upward_translation_table, precision=top_level_index
    )
    box_locals = leaf_far + downward_sent
    domain_local = lax.all_gather(box_locals, "blk", axis=0, tiled=True)
    block_locals = jnp.dot(box_hot, domain_local, precision=top_level_index)
    scaled = (bra_table.astype(jnp.float32) * block_locals[:, None, :]).astype(jnp.bfloat16)
    coulomb = jnp.einsum(
        "bmk,bnk->bmn", scaled, ket_table, preferred_element_type=jnp.float32
    ).astype(jnp.bfloat16)
    return (coulomb, box_locals)


def solution(mesh):
    placed = (
        P(("space", "blk"), None, None),
        P(("space", "blk"), None, None),
        P(("space", "blk"), None, None),
        P(("space", "blk")),
        P(("space", "blk"), None),
        P(("space", "blk"), None),
        P(("space", "blk"), None),
        P(("space", "blk"), None),
        P(),
        P(),
    )
    return jax.shard_map(
        shards,
        mesh=mesh,
        in_specs=placed,
        out_specs=(P(("space", "blk"), None, None), P(("space", "blk"), None)),
        check_vma=False,
    )
```

profile of v0, /device:TPU:1, one launch (start us, length us, event | category | flops | bytes accessed | tf_op | source)
XLA Modules:
  0.0 324.4 jit_solution(17972422086320185214)
XLA Ops:
  7.2 0.0 copy-start
  7.2 0.0 copy-start.6
  7.2 0.0 copy-start.8
  7.2 0.0 copy-start.7
  7.2 0.0 copy-start.5
  7.2 0.0 copy-start.4
  7.2 0.0 reduce-scatter.2.cloned.1.call-start
  7.3 1.8 copy-done
  9.1 6.8 %multiply_reduce_fusion = f32[96,256]{1,0:T(8,128)S(1)} fusion(bf16[96,128,256]{2,1,0:T(8,128)(2,1)} %param.12, bf16[96,128,128]{2,1,0:T(8,128)(2,1)S(1)} %copy-done, bf16[96,128,256]{2,1,0:T(8,128)(2,1)} %param.11), kind=kOutput, calls=%fused_computation.1 | convolution fusion | flops 814718976 | bytes 15826944 | tf_op jit(solution)/shard_map/bmn,bmk->bnk/dot_general | solution.py:36
  15.9 0.0 copy-done.6
  15.9 1.0 fusion.15
  16.9 0.0 reduce-scatter.2.cloned.1.call-update
  16.9 0.0 copy-done.8
  16.9 0.0 copy-done.7
  16.9 0.2 fusion.21
  17.1 0.0 copy-done.5
  17.1 0.0 copy-done.4
  17.1 0.2 fusion.9
  17.4 60.2 %reduce-scatter.2.cloned.1.call-done = f32[8,256]{1,0:T(8,128)} async-done(((f32[128,256]{1,0:T(8,128)}), f32[8,256]{1,0:T(8,128)}) %reduce-scatter.2.cloned.1.call-update) | async-done | bytes 8208 | tf_op jit(solution)/shard_map/reduce_scatter | solution.py:44
  77.6 0.0 copy-start.2
  77.6 0.0 copy-start.1
  77.6 20.7 %all_gather.9 = f32[128,256]{1,0:T(8,128)S(1)} all-gather(f32[8,256]{1,0:T(8,128)} %reduce-scatter.2.cloned.1.call-done), channel_id=1, replica_groups=mesh['space'=8,'blk'=16] {'blk'}, dimensions={0}, use_global_device_ids=true | all-gather | bytes 139264 | tf_op jit(solution)/shard_map/all_gather | solution.py:45
  98.3 1.3 collective-permute-start.1
  99.6 4.0 %collective-permute-start = (f32[128,256]{1,0:T(8,128)S(1)}, f32[128,256]{1,0:T(8,128)S(1)}, u32[]{:S(2)}, u32[]{:S(2)}) collective-permute-start(f32[128,256]{1,0:T(8,128)S(1)} %all_gather.9), channel_id=1, source_target_pairs={{0,16},{16,32},{32,48},{48,64},{64,80},{80,96},{96,112},{1,17},{17... | collective-permute-start | bytes 393224 | tf_op jit(solution)/shard_map/ppermute | solution.py:12
  103.6 3.3 %convolution_bitcast_fusion.3 = f32[1,1,256]{2,1,0:T(1,128)S(1)} fusion(f32[8,256,256]{2,1,0:T(8,128)} %param.19, f32[8,256,1]{1,0,2:T(8,128)} %bitcast.43), kind=kOutput, calls=%fused_computation.9 | convolution fusion | flops 6291456 | bytes 2106368 | tf_op jit(solution)/shard_map/oe,ode->d/dot_general | solution.py:47
  107.0 175.0 %all-gather.1 = f32[128,1,256]{2,1,0:T(1,128)S(1)} all-gather(f32[1,1,256]{2,1,0:T(1,128)S(1)} %convolution_bitcast_fusion.3), channel_id=2, replica_groups=mesh['space'=8,'blk'=16] {'space','blk'}, dimensions={0}, use_global_device_ids=true | all-gather | bytes 132096 | tf_op jit(solution)/shard_map/all_gather | solution.py:50
  282.0 0.2 convolution_bitcast_fusion
  282.1 5.5 %convolution_bitcast_fusion.2 = f32[256,1,1]{0,1,2:T(1,128)S(1)} fusion(f32[16,256,256]{2,1,0:T(8,128)} %param.18, f32[16,256,1]{1,0,2:T(8,128)S(1)} %convolution_bitcast_fusion), kind=kOutput, calls=%fused_computation.8 | convolution fusion | flops 12582912 | bytes 4211712 | tf_op jit(solution)/shard_map/ptk,tlk->pl/dot_general | solution.py:61
  287.7 0.0 copy-done.2
  287.7 1.1 fusion.29
  288.8 0.0 collective-permute-done.1
  288.8 0.0 collective-permute-done
  288.8 0.4 fusion.4
  289.2 0.0 copy-done.1
  289.2 3.3 %fusion.3 = f32[8,256]{1,0:T(8,128)S(1)} fusion(f32[8,16,256]{2,0,1:T(8,128)S(1)} %fusion.4, f32[16,256,256]{2,1,0:T(8,128)S(1)} %copy-done.1, f32[1,8,256]{2,0,1:T(1,128)S(1)} %fusion.29), kind=kOutput, calls=%fused_computation.7 | convolution fusion | flops 100665344 | bytes 4341760 | tf_op jit(solution)/shard_map/btk,tlk->bl/dot_general | solution.py:55
  292.6 0.0 copy-start.3
  292.6 16.6 %all_gather.11 = f32[128,256]{1,0:T(8,128)S(1)} all-gather(f32[8,256]{1,0:T(8,128)S(1)} %fusion.3), channel_id=1, replica_groups=mesh['space'=8,'blk'=16] {'blk'}, dimensions={0}, use_global_device_ids=true | all-gather | bytes 139264 | tf_op jit(solution)/shard_map/all_gather | solution.py:68
  309.2 0.2 fusion.14
  309.4 8.1 %fusion.2 = bf16[96,128,128]{2,1,0:T(8,128)(2,1)} fusion(bf16[96,128,256]{2,1,0:T(8,128)(2,1)} %param.12, bf16[96,128,256]{2,1,0:T(8,128)(2,1)} %param.11, f32[96,256]{1,0:T(8,128)S(1)} %fusion.14), kind=kOutput, calls=%fused_computation.4 | convolution fusion | flops 816316416 | bytes 15826944 | tf_op jit(solution)/shard_map/bmk,bnk->bmn/dot_general | solution.py:71
  317.5 0.0 copy-done.3
Async XLA Ops:
  7.2 1.9 copy-start
  7.2 8.7 %copy-start.6 = (s32[96]{0:T(128)S(1)}, s32[96]{0:T(128)}, u32[]{:S(2)}) copy-start(s32[96]{0:T(128)} %param.13) | copy-start | bytes 1156
  7.2 9.7 %copy-start.8 = (s32[1,27]{1,0:T(1,128)S(1)}, s32[1,27]{1,0:T(1,128)}, u32[]{:S(2)}) copy-start(s32[1,27]{1,0:T(1,128)} %param.17) | copy-start | bytes 328
  7.2 9.7 %copy-start.7 = (s32[1,27]{1,0:T(1,128)S(1)}, s32[1,27]{1,0:T(1,128)}, u32[]{:S(2)}) copy-start(s32[1,27]{1,0:T(1,128)} %param.16) | copy-start | bytes 328
  7.2 9.9 %copy-start.5 = (s32[8,27]{1,0:T(8,128)S(1)}, s32[8,27]{1,0:T(8,128)}, u32[]{:S(2)}) copy-start(s32[8,27]{1,0:T(8,128)} %param.15) | copy-start | bytes 2596
  7.2 9.9 %copy-start.4 = (s32[8,27]{1,0:T(8,128)S(1)}, s32[8,27]{1,0:T(8,128)}, u32[]{:S(2)}) copy-start(s32[8,27]{1,0:T(8,128)} %param.14) | copy-start | bytes 2596
  7.2 70.4 %reduce-scatter.2.cloned.1.call-start = ((), (), s32[]{:S(2)}) async-start(), calls=%async_computation.1 | async-start | bytes 139264 | tf_op jit(solution)/shard_map/reduce_scatter | solution.py:44
  77.6 210.1 %copy-start.2 = (f32[8,256,256]{2,1,0:T(8,128)S(1)}, f32[8,256,256]{2,1,0:T(8,128)}, u32[]{:S(2)}) copy-start(f32[8,256,256]{2,1,0:T(8,128)} %param.19) | copy-start | bytes 6291460
  77.6 211.6 %copy-start.1 = (f32[16,256,256]{2,1,0:T(8,128)S(1)}, f32[16,256,256]{2,1,0:T(8,128)}, u32[]{:S(2)}) copy-start(f32[16,256,256]{2,1,0:T(8,128)} %param.18) | copy-start | bytes 12582916
  98.3 190.5 %collective-permute-start.1 = (f32[128,256]{1,0:T(8,128)S(1)}, f32[128,256]{1,0:T(8,128)S(1)}, u32[]{:S(2)}, u32[]{:S(2)}) collective-permute-start(f32[128,256]{1,0:T(8,128)S(1)} %all_gather.9), channel_id=1, source_target_pairs={{16,0},{32,16},{48,32},{64,48},{80,64},{96,80},{112,96},{17,1},{33... | collective-permute-start | bytes 393224 | tf_op jit(solution)/shard_map/ppermute | solution.py:15
  99.6 189.2 %collective-permute-start = (f32[128,256]{1,0:T(8,128)S(1)}, f32[128,256]{1,0:T(8,128)S(1)}, u32[]{:S(2)}, u32[]{:S(2)}) collective-permute-start(f32[128,256]{1,0:T(8,128)S(1)} %all_gather.9), channel_id=1, source_target_pairs={{0,16},{16,32},{32,48},{48,64},{64,80},{80,96},{96,112},{1,17},{17... | collective-permute-start | bytes 393224 | tf_op jit(solution)/shard_map/ppermute | solution.py:12
  292.6 24.9 %copy-start.3 = (f32[8,256]{1,0:T(8,128)}, f32[8,256]{1,0:T(8,128)S(1)}, u32[]{:S(2)}) copy-start(f32[8,256]{1,0:T(8,128)S(1)} %fusion.3) | copy-start | bytes 24580
Sparse Core Ops, SparseCore 0:
  17.0 60.5 reduce-scatter.1
where the time goes:
time: 325 us; the launch traced here: 324 us
  blocking collectives  212 us (65%)
  waiting for transfers between devices  60.3 us (19%)
  matrix products  30.5 us (9%)
  between operations  14.2 us (4%)
  starting transfers between devices  5.31 us (2%)
    all_gather x1, blocking collectives, shards(): lax.all_gather(self_parent_index, ('space', 'blk'), axis=0, tiled=True)  175 us
    reduce_scatter x1, waiting for transfers between devices, shards(): lax.psum_scatter(partial_moments, 'blk', scatter_dimension=0, tiled=True)  60.2 us
    all_gather x1, blocking collectives, shards(): domain = lax.all_gather(held_boxes, 'blk', axis=0, tiled=True)  20.7 us
    all_gather x1, blocking collectives, shards(): domain_local = lax.all_gather(box_locals, 'blk', axis=0, tiled=True)  16.6 us
    dot_general x1, matrix products, shards(): jnp.einsum('bmk,bnk->bmn', scaled, ket_table, preferred_element_type=jnp....  8.08 us
    dot_general x1, matrix products, shards(): jnp.einsum('bmn,bmk->bnk', density, bra_table, preferred_element_type=jnp...  6.82 us
  transfers between devices with their start and end apart: 3, of which 1 were waited for; matrix products, arithmetic and copies ran while one was open for 3% of the time, Pallas kernels for 0%

commit v1 on v0

--- a/solution.py
+++ b/solution.py
@@ -47,7 +47,12 @@
     self_parent_index = jnp.einsum(
         "oe,ode->d", held_boxes, upward_translation_table, precision=top_level_index
     )[None, :]
-    all_parents = lax.all_gather(self_parent_index, ("space", "blk"), axis=0, tiled=True)
+    all_parents = jnp.concatenate(
+        lax.all_to_all(
+            jnp.stack([self_parent_index] * lax.axis_size(("space", "blk"))), ("space", "blk"), 0, 0
+        ),
+        axis=0,
+    )
     src_hot = (leaf_src[..., None] == jnp.arange(3 * box_dom, dtype=jnp.int32)).astype(jnp.float32)
     type_hot = (leaf_type[..., None] == jnp.arange(n_types, dtype=jnp.int32)).astype(jnp.float32)
     counts = jnp.einsum("blt,blj->btj", type_hot, src_hot, precision=top_level_index)

time: 325 us -> 169 us (0.52)
  blocking collectives: 212 us -> 39 us
  starting transfers between devices: 5.31 us -> 16.5 us
    all_gather x1 -> x0, blocking collectives: 175 us -> none  [shards(): lax.all_gather(self_parent_index, ('space', 'blk'), axis=0, tiled=True)]
    all_to_all x0 -> x1, starting transfers between devices: none -> 10.5 us  [shards(): lax.all_to_all(jnp.stack([self_parent_index] * lax.axis_size(('space', 'b...]
  transfers between devices with their start and end apart: 3 -> 4, of which waited for: 1 -> 1; matrix products, arithmetic and copies ran while one was open for 3% -> 5% of each run, Pallas kernels for 0% -> 0%
where the time goes in v1:
time: 169 us; the launch traced here: 166 us
  waiting for transfers between devices  60.4 us (36%)
  blocking collectives  39 us (23%)
  matrix products  33.3 us (20%)
  starting transfers between devices  16.5 us (10%)
  between operations  14.2 us (8%)
  local copies, waits for them, and re-layouts  2.56 us (2%)
    reduce_scatter x1, waiting for transfers between devices, shards(): lax.psum_scatter(partial_moments, 'blk', scatter_dimension=0, tiled=True)  60.4 us
    all_gather x1, blocking collectives, shards(): domain = lax.all_gather(held_boxes, 'blk', axis=0, tiled=True)  22.2 us
    all_gather x1, blocking collectives, shards(): domain_local = lax.all_gather(box_locals, 'blk', axis=0, tiled=True)  16.9 us
    all_to_all x1, starting transfers between devices, shards(): lax.all_to_all(jnp.stack([self_parent_index] * lax.axis_size(('space', 'b...  10.5 us
    dot_general x1, matrix products, shards(): jnp.einsum('bmk,bnk->bmn', scaled, ket_table, preferred_element_type=jnp....  8.08 us
    dot_general x1, matrix products, shards(): jnp.einsum('bmn,bmk->bnk', density, bra_table, preferred_element_type=jnp...  6.82 us
    dot_general x1, matrix products, shards(): jnp.einsum('ptk,tlk->pl', cgathered, translation, precision=top_level_index)  5.7 us
    ppermute x1, starting transfers between devices, padded(): lax.ppermute(lax.slice_in_dim(block, block.shape[dim] - width, None, axis...  4.64 us
  transfers between devices with their start and end apart: 4, of which 1 were waited for; matrix products, arithmetic and copies ran while one was open for 5% of the time, Pallas kernels for 0%

profile of v1, /device:TPU:1, one launch (start us, length us, event | category | flops | bytes accessed | tf_op | source)
XLA Modules:
  0.0 166.0 jit_solution(4582340891237530754)
XLA Ops:
  7.2 0.0 copy-start
  7.2 0.0 copy-start.5
  7.2 0.0 copy-start.4
  7.2 0.0 copy-start.3
  7.2 0.0 copy-start.7
  7.2 0.0 copy-start.6
  7.2 0.0 reduce-scatter.2.cloned.1.call-start
  7.3 1.8 %copy-done = bf16[96,128,128]{2,1,0:T(8,128)(2,1)S(1)} copy-done((bf16[96,128,128]{2,1,0:T(8,128)(2,1)S(1)}, bf16[96,128,128]{2,1,0:T(8,128)(2,1)}, u32[]{:S(2)}) %copy-start) | copy-done | bytes 3145752
  9.1 6.8 %multiply_reduce_fusion = f32[96,256]{1,0:T(8,128)S(1)} fusion(bf16[96,128,256]{2,1,0:T(8,128)(2,1)} %param.12, bf16[96,128,128]{2,1,0:T(8,128)(2,1)S(1)} %copy-done, bf16[96,128,256]{2,1,0:T(8,128)(2,1)} %param.11), kind=kOutput, calls=%fused_computation.1 | convolution fusion | flops 814718976 | bytes 15826944 | tf_op jit(solution)/shard_map/bmn,bmk->bnk/dot_general | solution.py:36
  15.9 0.0 copy-done.5
  15.9 1.0 fusion.16
  16.9 0.0 reduce-scatter.2.cloned.1.call-update
  16.9 0.0 copy-done.4
  16.9 0.0 copy-done.3
  16.9 0.3 fusion.9
  17.3 60.4 %reduce-scatter.2.cloned.1.call-done = f32[8,256]{1,0:T(8,128)} async-done(((f32[128,256]{1,0:T(8,128)}), f32[8,256]{1,0:T(8,128)}) %reduce-scatter.2.cloned.1.call-update) | async-done | bytes 8208 | tf_op jit(solution)/shard_map/reduce_scatter | solution.py:44
  77.6 3.3 %fusion.23 = f32[1,256,1]{1,0,2:T(1,128)S(1)} fusion(f32[8,256,256]{2,1,0:T(8,128)} %param.19, f32[8,256,1]{1,0,2:T(8,128)} %bitcast.40), kind=kOutput, calls=%fused_computation.32 | convolution fusion | flops 6291456 | bytes 2106368 | tf_op jit(solution)/shard_map/oe,ode->d/dot_general | solution.py:47
  80.9 0.7 stack.3
  81.7 10.5 %all-to-all-start = ((f32[128,1,256]{2,1,0:T(1,128)}), f32[128,1,256]{2,1,0:T(1,128)S(1)}, u32[]{:S(2)}, u32[]{:S(2)}) async-start(f32[128,1,256]{2,1,0:T(1,128)} %stack.3), calls=%async_computation.1 | async-start | bytes 262144 | tf_op jit(solution)/shard_map/all_to_all | solution.py:51
  92.2 0.0 copy-done.7
  92.2 0.0 copy-done.6
  92.3 0.2 fusion.21
  92.4 22.2 %all_gather.6 = f32[128,256]{1,0:T(8,128)} all-gather(f32[8,256]{1,0:T(8,128)} %reduce-scatter.2.cloned.1.call-done), channel_id=1, replica_groups=mesh['space'=8,'blk'=16] {'blk'}, dimensions={0}, use_global_device_ids=true | all-gather | bytes 139264 | tf_op jit(solution)/shard_map/all_gather | solution.py:45
  114.6 1.3 collective-permute-start.1
  115.9 4.6 %collective-permute-start = (f32[128,256]{1,0:T(8,128)}, f32[128,256]{1,0:T(8,128)}, u32[]{:S(2)}, u32[]{:S(2)}) collective-permute-start(f32[128,256]{1,0:T(8,128)} %all_gather.6), channel_id=1, source_target_pairs={{0,16},{16,32},{32,48},{48,64},{64,80},{80,96},{96,112},{1,17},{17... | collective-permute-start | bytes 393224 | tf_op jit(solution)/shard_map/ppermute | solution.py:12
  120.5 0.0 all-to-all-done
  120.6 0.0 copy-start.1
  120.6 0.2 convolution_bitcast_fusion
  120.7 5.7 %convolution_bitcast_fusion.2 = f32[256,1,1]{0,1,2:T(1,128)S(1)} fusion(f32[16,256,256]{2,1,0:T(8,128)} %param.18, f32[16,256,1]{1,0,2:T(8,128)S(1)} %convolution_bitcast_fusion), kind=kOutput, calls=%fused_computation.8 | convolution fusion | flops 12582912 | bytes 4211712 | tf_op jit(solution)/shard_map/ptk,tlk->pl/dot_general | solution.py:66
  126.4 2.7 %fusion.30 = f32[1,8,256]{2,0,1:T(1,128)S(1)} fusion(f32[256,1,1]{0,1,2:T(1,128)S(1)} %convolution_bitcast_fusion.2, f32[8,256,256]{2,1,0:T(8,128)} %param.19), kind=kOutput, calls=%fused_computation.39 | convolution fusion | flops 6291456 | bytes 2106368 | tf_op jit(solution)/shard_map/d,uds->us/dot_general | solution.py:69
  129.1 0.0 collective-permute-done.1
  129.1 0.0 collective-permute-done
  129.1 1.4 fusion.4
  130.6 0.0 copy-done.1
  130.6 3.3 %fusion.3 = f32[8,256]{1,0:T(8,128)S(1)} fusion(f32[8,16,256]{2,0,1:T(8,128)S(1)} %fusion.4, f32[16,256,256]{2,1,0:T(8,128)S(1)} %copy-done.1, f32[1,8,256]{2,0,1:T(1,128)S(1)} %fusion.30), kind=kOutput, calls=%fused_computation.7 | convolution fusion | flops 100665344 | bytes 4341760 | tf_op jit(solution)/shard_map/btk,tlk->bl/dot_general | solution.py:60
  133.9 0.0 copy-start.2
  133.9 16.9 %all_gather.7 = f32[128,256]{1,0:T(8,128)S(1)} all-gather(f32[8,256]{1,0:T(8,128)S(1)} %fusion.3), channel_id=1, replica_groups=mesh['space'=8,'blk'=16] {'blk'}, dimensions={0}, use_global_device_ids=true | all-gather | bytes 139264 | tf_op jit(solution)/shard_map/all_gather | solution.py:73
  150.8 0.2 fusion.15
  151.0 8.1 %fusion.2 = bf16[96,128,128]{2,1,0:T(8,128)(2,1)} fusion(bf16[96,128,256]{2,1,0:T(8,128)(2,1)} %param.12, bf16[96,128,256]{2,1,0:T(8,128)(2,1)} %param.11, f32[96,256]{1,0:T(8,128)S(1)} %fusion.15), kind=kOutput, calls=%fused_computation.4 | convolution fusion | flops 816316416 | bytes 15826944 | tf_op jit(solution)/shard_map/bmk,bnk->bmn/dot_general | solution.py:76
  159.1 0.0 copy-done.2
Async XLA Ops:
  7.2 1.9 %copy-start = (bf16[96,128,128]{2,1,0:T(8,128)(2,1)S(1)}, bf16[96,128,128]{2,1,0:T(8,128)(2,1)}, u32[]{:S(2)}) copy-start(bf16[96,128,128]{2,1,0:T(8,128)(2,1)} %param.10) | copy-start | bytes 9437188
  7.2 8.7 %copy-start.5 = (s32[96]{0:T(128)S(1)}, s32[96]{0:T(128)}, u32[]{:S(2)}) copy-start(s32[96]{0:T(128)} %param.13) | copy-start | bytes 1156
  7.2 9.7 %copy-start.4 = (s32[8,27]{1,0:T(8,128)S(1)}, s32[8,27]{1,0:T(8,128)}, u32[]{:S(2)}) copy-start(s32[8,27]{1,0:T(8,128)} %param.15) | copy-start | bytes 2596
  7.2 9.7 %copy-start.3 = (s32[8,27]{1,0:T(8,128)S(1)}, s32[8,27]{1,0:T(8,128)}, u32[]{:S(2)}) copy-start(s32[8,27]{1,0:T(8,128)} %param.14) | copy-start | bytes 2596
  7.2 85.0 %copy-start.7 = (s32[1,27]{1,0:T(1,128)S(1)}, s32[1,27]{1,0:T(1,128)}, u32[]{:S(2)}) copy-start(s32[1,27]{1,0:T(1,128)} %param.17) | copy-start | bytes 328
  7.2 85.0 %copy-start.6 = (s32[1,27]{1,0:T(1,128)S(1)}, s32[1,27]{1,0:T(1,128)}, u32[]{:S(2)}) copy-start(s32[1,27]{1,0:T(1,128)} %param.16) | copy-start | bytes 328
  7.2 70.4 %reduce-scatter.2.cloned.1.call-start = ((), (), s32[]{:S(2)}) async-start(), calls=%async_computation.2 | async-start | bytes 139264 | tf_op jit(solution)/shard_map/reduce_scatter | solution.py:44
  81.7 38.9 %all-to-all-start = ((f32[128,1,256]{2,1,0:T(1,128)}), f32[128,1,256]{2,1,0:T(1,128)S(1)}, u32[]{:S(2)}, u32[]{:S(2)}) async-start(f32[128,1,256]{2,1,0:T(1,128)} %stack.3), calls=%async_computation.1 | async-start | bytes 262144 | tf_op jit(solution)/shard_map/all_to_all | solution.py:51
  114.6 14.5 %collective-permute-start.1 = (f32[128,256]{1,0:T(8,128)}, f32[128,256]{1,0:T(8,128)}, u32[]{:S(2)}, u32[]{:S(2)}) collective-permute-start(f32[128,256]{1,0:T(8,128)} %all_gather.6), channel_id=1, source_target_pairs={{16,0},{32,16},{48,32},{64,48},{80,64},{96,80},{112,96},{17,1},{33... | collective-permute-start | bytes 393224 | tf_op jit(solution)/shard_map/ppermute | solution.py:15
  115.9 13.2 %collective-permute-start = (f32[128,256]{1,0:T(8,128)}, f32[128,256]{1,0:T(8,128)}, u32[]{:S(2)}, u32[]{:S(2)}) collective-permute-start(f32[128,256]{1,0:T(8,128)} %all_gather.6), channel_id=1, source_target_pairs={{0,16},{16,32},{32,48},{48,64},{64,80},{80,96},{96,112},{1,17},{17... | collective-permute-start | bytes 393224 | tf_op jit(solution)/shard_map/ppermute | solution.py:12
  120.6 10.0 %copy-start.1 = (f32[16,256,256]{2,1,0:T(8,128)S(1)}, f32[16,256,256]{2,1,0:T(8,128)}, u32[]{:S(2)}) copy-start(f32[16,256,256]{2,1,0:T(8,128)} %param.18) | copy-start | bytes 12582916
  133.9 25.2 %copy-start.2 = (f32[8,256]{1,0:T(8,128)}, f32[8,256]{1,0:T(8,128)S(1)}, u32[]{:S(2)}) copy-start(f32[8,256]{1,0:T(8,128)S(1)} %fusion.3) | copy-start | bytes 24580
Sparse Core Ops, SparseCore 0:
  17.0 60.5 reduce-scatter.1
